TPU v7x, 32 devices: a whole 2x2x4 slice. The times are simulated.
32 devices in a mesh: pair: 4 (over z), src: 2 (over x), tgt: 4 (over y, core).
Axes of the slice: x: 2, y: 2, z: 4, core: 2. Of those that a mesh axis runs over, the one named last changes fastest.
Arguments:
- src_cells: float32 [4, 30, 4096], P('pair', None, 'src'), may hold values from -17 to 17
- final_cells: float32 [30, 4096], P(None, 'tgt'), may hold values from -17 to 17
- growth: float32 [4, 4096], P('pair', 'src'), may hold values from 0.5 to 2
- live: int32 [5], replicated, may hold values from 1024 to 4096, as said below
- final_fates: float32 [40, 4096], P(None, 'tgt'), may hold values from 0 to 1
Outputs:
- fate_maps: float32 [4, 40, 4096], P('pair', None, ('src', 'tgt'))
- potentials: float32 [4, 4096], P('pair', 'src')
Inputs may be any that keep to these rules, and one draw needn't show every extreme that they name: `live`: every count is at least 1024 and one snapshot fills all 4096 slots.
All inputs are finite; a program needn't handle non-finite values.
Results may differ from a plain program's by a relative error of at most 0.0049.
Values may be sent and summed in bfloat16 or wider, within the bound.
No kernel may reach another device: no remote copies, remote signals or barrier semaphores. Data moves between devices by JAX's collectives and lax.ppermute only.
A program may use at most 64 MiB of HBM per device.

v0:
```python
import jax
import jax.numpy as jnp
from jax import lax
from jax.sharding import PartitionSpec as P

ITERS = 8
EPS = 0.1
LAM = 1.0
NEG = -1e30


def joined(shard, axis, combine):
    everything = jax.tree.map(lambda part: lax.all_gather(part, axis), shard)
    leading = jax.tree.map(lambda part: part[0], everything)

    def step(k, so_far):
        return combine(so_far, jax.tree.map(lambda part: part[k], everything))

    return lax.fori_loop(1, lax.axis_size(axis), step, leading)


def shifted(shard, axis, by):
    devices = lax.axis_size(axis)
    pairs = [(i, i + by) for i in range(devices) if 0 <= i + by < devices]
    return lax.ppermute(shard, axis, pairs)


def from_root(shard, axis, root):
    mine = lax.axis_index(axis) == root
    return lax.psum(jnp.where(mine, shard, jnp.zeros_like(shard)), axis)


def combine(first, second):
    peak = jnp.maximum(first[0], second[0])
    return (peak, first[1] * jnp.exp(first[0] - peak) + second[1] * jnp.exp(second[0] - peak))


def column_lse(col_scores):
    peak = jnp.max(col_scores, axis=0)
    totals = jnp.sum(jnp.exp(col_scores - peak[None, :]), axis=0)
    return joined((peak, totals), "src", combine)


def row_lse(row_scores):
    peak = jnp.max(row_scores, axis=1)
    totals = jnp.sum(jnp.exp(row_scores - peak[:, None]), axis=1)
    return joined((peak, totals), "tgt", combine)


def local(src_cells, final_cells, growth, live, final_fates):
    pair_count = lax.axis_size("pair")
    src_count = lax.axis_size("src")
    tgt_count = lax.axis_size("tgt")
    pair_rank = lax.axis_index("pair")
    src_rank = lax.axis_index("src")
    tgt_rank = lax.axis_index("tgt")
    shrink = LAM / (LAM + EPS)
    source_pos = src_cells[0]
    src_width = source_pos.shape[1]
    tgt_width = final_cells.shape[1]
    share_width = src_width // tgt_count
    tgt_ratio = tgt_count // src_count
    owner_rank = tgt_rank // tgt_ratio
    offset_in = tgt_rank % tgt_ratio * tgt_width
    is_last = pair_rank == pair_count - 1
    arrived = shifted(source_pos, "pair", -1)
    owner_cells = from_root(arrived, "src", owner_rank)
    target_pos = jnp.where(
        is_last, final_cells, lax.dynamic_slice_in_dim(owner_cells, offset_in, tgt_width, 1)
    )
    cross = lax.dot_general(
        source_pos,
        target_pos,
        (((0,), (0,)), ((), ())),
        precision=lax.Precision.HIGHEST,
        preferred_element_type=jnp.float32,
    )
    src_sq = jnp.sum(source_pos * source_pos, axis=0)
    tgt_sq = jnp.sum(target_pos * target_pos, axis=0)
    cost_tile = (src_sq[:, None] + tgt_sq[None, :] - 2.0 * cross) / (2.0 * source_pos.shape[0])
    live_now = lax.dynamic_index_in_dim(live, pair_rank, keepdims=False)
    live_next = lax.dynamic_index_in_dim(live, pair_rank + 1, keepdims=False)
    src_index = src_rank * src_width + jnp.arange(src_width, dtype=jnp.int32)
    tgt_index = tgt_rank * tgt_width + jnp.arange(tgt_width, dtype=jnp.int32)
    share_index = (src_rank * tgt_count + tgt_rank) * share_width + jnp.arange(
        share_width, dtype=jnp.int32
    )
    live_src = src_index < live_now
    live_tgt = tgt_index < live_next
    live_share = share_index < live_now
    log_mass_a = jnp.where(
        live_src, jnp.log(growth[0]) - jnp.log(live_now.astype(jnp.float32)), NEG
    )
    log_mass_b = jnp.where(
        live_tgt, -jnp.log(live_next.astype(jnp.float32)) * jnp.ones((tgt_width,), jnp.float32), NEG
    )
    pot_src = jnp.zeros((src_width,), jnp.float32)
    pot_tgt = jnp.zeros((tgt_width,), jnp.float32)
    for step_num in range(ITERS):
        col_scores = (pot_src[:, None] - cost_tile) / EPS + log_mass_a[:, None]
        col_peak, col_total = column_lse(col_scores)
        pot_tgt = -shrink * EPS * (col_peak + jnp.log(col_total))
        row_scores = (pot_tgt[None, :] - cost_tile) / EPS + log_mass_b[None, :]
        row_peak, row_total = row_lse(row_scores)
        pot_src = -shrink * EPS * (row_peak + jnp.log(row_total))
    weights = (jnp.exp(row_scores - row_peak[:, None]) / row_total[:, None]).astype(jnp.bfloat16)
    handed = jnp.where(
        is_last, final_fates.astype(jnp.bfloat16), jnp.zeros(final_fates.shape, jnp.bfloat16)
    )
    fate_maps = jnp.zeros((final_fates.shape[0], share_width), jnp.float32)
    for section_num in range(pair_count):
        active = pair_count - 1 - section_num
        partial_value = lax.dot_general(
            handed, weights, (((1,), (1,)), ((), ())), preferred_element_type=jnp.float32
        )
        fate_share = lax.psum_scatter(partial_value, "tgt", scatter_dimension=1, tiled=True)
        fate_share = jnp.where(live_share[None, :], fate_share, 0.0)
        fate_maps = jnp.where(pair_rank == active, fate_share, fate_maps)
        if section_num + 1 < pair_count:
            passed = shifted(fate_share.astype(jnp.bfloat16), "pair", -1)
            gathered = lax.all_gather(passed, ("src", "tgt"), axis=1, tiled=True)
            fresh = lax.dynamic_slice_in_dim(gathered, tgt_rank * tgt_width, tgt_width, 1)
            handed = jnp.where(pair_rank == active - 1, fresh, handed)
    return (fate_maps[None], pot_src[None])


def solution(mesh):
    placed = (P("pair", None, "src"), P(None, "tgt"), P("pair", "src"), P(), P(None, "tgt"))
    return jax.shard_map(
        local,
        mesh=mesh,
        in_specs=placed,
        out_specs=(P("pair", None, ("src", "tgt")), P("pair", "src")),
        check_vma=False,
    )
```

profile of v0, /device:TPU:0, one launch (start us, length us, event | category | flops | bytes accessed | tf_op | source)
XLA Modules:
  0.0 468.3 jit_solution(16337164708790287307)
XLA Ops:
  14.0 5.5 %collective-permute-done = f32[30,2048]{1,0:T(8,128)S(1)} collective-permute-done((f32[30,2048]{1,0:T(8,128)S(1)}, f32[30,2048]{1,0:T(8,128)S(1)}, u32[]{:S(2)}, u32[]{:S(2)}) %collective-permute-start) | collective-permute-done | bytes 245792 | tf_op jit(solution)/shard_map/ppermute | solution.py:25
  21.6 22.5 %all-reduce.2.cloned.1.call-done = f32[30,2048]{1,0:T(8,128)} async-done(((f32[30,2048]{1,0:T(8,128)}), f32[30,2048]{1,0:T(8,128)}) %all-reduce.2.cloned.1.call-update) | async-done | bytes 245776 | tf_op jit(solution)/shard_map/psum | solution.py:30
  45.0 10.0 %fusion.1 = (f32[1024]{0:T(1024)S(1)}, f32[2048,1024]{0,1:T(8,128)S(1)}) fusion(f32[2048]{0:T(1024)S(1)} %fusion.23, f32[1,30,2048]{2,0,1:T(1,128)} %param.21, f32[30,1024]{1,0:T(8,128)} %param.22, f32[30,2048]{1,0:T(8,128)} %all-reduce.2.cloned.1.call-done, s32[]{:T(128)S(6)} %select_n.247, pred[]{:T(512)S(6)} %eq.24, f32[1024]{0:T(1024)S(1)} %multiply_reduce_fusion.1, ...), kind=kOutput, calls=%fused_computation.59 | convolution fusion | flops 771781632 | bytes 8921093 | tf_op jit(solution)/shard_map/dot_general | solution.py:71
  55.0 4.4 all-gather
  59.4 2.5 exponential_reduce_fusion.15
  61.8 4.5 all-gather.1
  70.1 5.2 %all-gather.2 = f32[8192]{0:T(1024)S(1)} all-gather(f32[2048]{0:T(1024)S(1)} %fusion.2), channel_id=4, replica_groups=mesh['pair'=4,'src'=2,'tgt'=4] {'tgt'}, dimensions={0}, use_global_device_ids=true | all-gather | bytes 40960 | tf_op jit(solution)/shard_map/all_gather | solution.py:13
  75.3 5.2 %all-gather.3 = f32[8192]{0:T(1024)S(1)} all-gather(f32[2048]{0:T(1024)S(1)} %exponential_reduce_fusion.14), channel_id=5, replica_groups=mesh['pair'=4,'src'=2,'tgt'=4] {'tgt'}, dimensions={0}, use_global_device_ids=true | all-gather | bytes 40960 | tf_op jit(solution)/shard_map/all_gather | solution.py:13
  80.7 4.7 %fusion.3 = f32[1024]{0:T(1024)S(1)} fusion(f32[2048,1024]{0,1:T(8,128)} %copy-done, f32[2048]{0:T(1024)S(1)} %add_multiply_fusion.7, f32[2048]{0:T(1024)S(1)} %fusion.23), kind=kLoop, calls=%fused_computation.61 | loop fusion | flops 8387584 | bytes 8409088 | tf_op jit(solution)/shard_map/reduce_max | solution.py:39
  86.4 2.5 exponential_reduce_fusion.13
  88.9 4.4 all-gather.4
  93.3 4.3 all-gather.5
  101.3 5.2 %all-gather.6 = f32[8192]{0:T(1024)S(1)} all-gather(f32[2048]{0:T(1024)S(1)} %fusion.4), channel_id=8, replica_groups=mesh['pair'=4,'src'=2,'tgt'=4] {'tgt'}, dimensions={0}, use_global_device_ids=true | all-gather | bytes 40960 | tf_op jit(solution)/shard_map/all_gather | solution.py:13
  106.5 5.2 %all-gather.7 = f32[8192]{0:T(1024)S(1)} all-gather(f32[2048]{0:T(1024)S(1)} %exponential_reduce_fusion.12), channel_id=9, replica_groups=mesh['pair'=4,'src'=2,'tgt'=4] {'tgt'}, dimensions={0}, use_global_device_ids=true | all-gather | bytes 40960 | tf_op jit(solution)/shard_map/all_gather | solution.py:13
  112.0 4.7 %fusion.5 = f32[1024]{0:T(1024)S(1)} fusion(f32[2048,1024]{0,1:T(8,128)} %copy-done, f32[2048]{0:T(1024)S(1)} %add_multiply_fusion.6, f32[2048]{0:T(1024)S(1)} %fusion.23), kind=kLoop, calls=%fused_computation.63 | loop fusion | flops 8387584 | bytes 8409088 | tf_op jit(solution)/shard_map/reduce_max | solution.py:39
  116.7 5.3 %exponential_reduce_fusion.11 = f32[1024]{0:T(1024)S(1)} fusion(f32[2048,1024]{0,1:T(8,128)} %copy-done, f32[1024]{0:T(1024)S(1)} %fusion.5, f32[2048]{0:T(1024)S(1)} %add_multiply_fusion.6, f32[2048]{0:T(1024)S(1)} %fusion.23), kind=kLoop, calls=%fused_computation.49 | loop fusion | flops 10484736 | bytes 8413184 | tf_op jit(solution)/shard_map/reduce_sum | solution.py:40
  122.0 4.4 all-gather.8
  126.4 4.6 all-gather.9
  134.7 5.2 %all-gather.10 = f32[8192]{0:T(1024)S(1)} all-gather(f32[2048]{0:T(1024)S(1)} %fusion.6), channel_id=12, replica_groups=mesh['pair'=4,'src'=2,'tgt'=4] {'tgt'}, dimensions={0}, use_global_device_ids=true | all-gather | bytes 40960 | tf_op jit(solution)/shard_map/all_gather | solution.py:13
  139.9 5.2 %all-gather.11 = f32[8192]{0:T(1024)S(1)} all-gather(f32[2048]{0:T(1024)S(1)} %exponential_reduce_fusion.10), channel_id=13, replica_groups=mesh['pair'=4,'src'=2,'tgt'=4] {'tgt'}, dimensions={0}, use_global_device_ids=true | all-gather | bytes 40960 | tf_op jit(solution)/shard_map/all_gather | solution.py:13
  145.3 4.7 %fusion.7 = f32[1024]{0:T(1024)S(1)} fusion(f32[2048,1024]{0,1:T(8,128)} %copy-done, f32[2048]{0:T(1024)S(1)} %add_multiply_fusion.5, f32[2048]{0:T(1024)S(1)} %fusion.23), kind=kLoop, calls=%fused_computation.65 | loop fusion | flops 8387584 | bytes 8409088 | tf_op jit(solution)/shard_map/reduce_max | solution.py:39
  150.1 5.3 %exponential_reduce_fusion.9 = f32[1024]{0:T(1024)S(1)} fusion(f32[2048,1024]{0,1:T(8,128)} %copy-done, f32[1024]{0:T(1024)S(1)} %fusion.7, f32[2048]{0:T(1024)S(1)} %add_multiply_fusion.5, f32[2048]{0:T(1024)S(1)} %fusion.23), kind=kLoop, calls=%fused_computation.45 | loop fusion | flops 10484736 | bytes 8413184 | tf_op jit(solution)/shard_map/reduce_sum | solution.py:40
  155.4 4.4 all-gather.12
  159.8 4.3 all-gather.13
  167.8 5.2 %all-gather.14 = f32[8192]{0:T(1024)S(1)} all-gather(f32[2048]{0:T(1024)S(1)} %fusion.8), channel_id=16, replica_groups=mesh['pair'=4,'src'=2,'tgt'=4] {'tgt'}, dimensions={0}, use_global_device_ids=true | all-gather | bytes 40960 | tf_op jit(solution)/shard_map/all_gather | solution.py:13
  173.1 5.2 %all-gather.15 = f32[8192]{0:T(1024)S(1)} all-gather(f32[2048]{0:T(1024)S(1)} %exponential_reduce_fusion.8), channel_id=17, replica_groups=mesh['pair'=4,'src'=2,'tgt'=4] {'tgt'}, dimensions={0}, use_global_device_ids=true | all-gather | bytes 40960 | tf_op jit(solution)/shard_map/all_gather | solution.py:13
  178.5 4.7 %fusion.9 = f32[1024]{0:T(1024)S(1)} fusion(f32[2048,1024]{0,1:T(8,128)} %copy-done, f32[2048]{0:T(1024)S(1)} %add_multiply_fusion.4, f32[2048]{0:T(1024)S(1)} %fusion.23), kind=kLoop, calls=%fused_computation.67 | loop fusion | flops 8387584 | bytes 8409088 | tf_op jit(solution)/shard_map/reduce_max | solution.py:39
  183.2 5.3 %exponential_reduce_fusion.7 = f32[1024]{0:T(1024)S(1)} fusion(f32[2048,1024]{0,1:T(8,128)} %copy-done, f32[1024]{0:T(1024)S(1)} %fusion.9, f32[2048]{0:T(1024)S(1)} %add_multiply_fusion.4, f32[2048]{0:T(1024)S(1)} %fusion.23), kind=kLoop, calls=%fused_computation.41 | loop fusion | flops 10484736 | bytes 8413184 | tf_op jit(solution)/shard_map/reduce_sum | solution.py:40
  188.6 4.4 all-gather.16
  192.9 4.8 %all-gather.17 = f32[2048]{0:T(1024)S(1)} all-gather(f32[1024]{0:T(1024)S(1)} %exponential_reduce_fusion.7), channel_id=19, replica_groups=mesh['pair'=4,'src'=2,'tgt'=4] {'src'}, dimensions={0}, use_global_device_ids=true | all-gather | bytes 12288 | tf_op jit(solution)/shard_map/all_gather | solution.py:13
  201.4 5.2 %all-gather.18 = f32[8192]{0:T(1024)S(1)} all-gather(f32[2048]{0:T(1024)S(1)} %fusion.10), channel_id=20, replica_groups=mesh['pair'=4,'src'=2,'tgt'=4] {'tgt'}, dimensions={0}, use_global_device_ids=true | all-gather | bytes 40960 | tf_op jit(solution)/shard_map/all_gather | solution.py:13
  206.6 5.2 %all-gather.19 = f32[8192]{0:T(1024)S(1)} all-gather(f32[2048]{0:T(1024)S(1)} %exponential_reduce_fusion.6), channel_id=21, replica_groups=mesh['pair'=4,'src'=2,'tgt'=4] {'tgt'}, dimensions={0}, use_global_device_ids=true | all-gather | bytes 40960 | tf_op jit(solution)/shard_map/all_gather | solution.py:13
  212.1 4.7 %fusion.11 = f32[1024]{0:T(1024)S(1)} fusion(f32[2048,1024]{0,1:T(8,128)} %copy-done, f32[2048]{0:T(1024)S(1)} %add_multiply_fusion.3, f32[2048]{0:T(1024)S(1)} %fusion.23), kind=kLoop, calls=%fused_computation.69 | loop fusion | flops 8387584 | bytes 8409088 | tf_op jit(solution)/shard_map/reduce_max | solution.py:39
  216.8 5.3 %exponential_reduce_fusion.5 = f32[1024]{0:T(1024)S(1)} fusion(f32[2048,1024]{0,1:T(8,128)} %copy-done, f32[1024]{0:T(1024)S(1)} %fusion.11, f32[2048]{0:T(1024)S(1)} %add_multiply_fusion.3, f32[2048]{0:T(1024)S(1)} %fusion.23), kind=kLoop, calls=%fused_computation.37 | loop fusion | flops 10484736 | bytes 8413184 | tf_op jit(solution)/shard_map/reduce_sum | solution.py:40
  222.2 4.4 all-gather.20
  226.5 4.3 all-gather.21
  234.6 5.2 %all-gather.22 = f32[8192]{0:T(1024)S(1)} all-gather(f32[2048]{0:T(1024)S(1)} %fusion.12), channel_id=24, replica_groups=mesh['pair'=4,'src'=2,'tgt'=4] {'tgt'}, dimensions={0}, use_global_device_ids=true | all-gather | bytes 40960 | tf_op jit(solution)/shard_map/all_gather | solution.py:13
  239.8 5.2 %all-gather.23 = f32[8192]{0:T(1024)S(1)} all-gather(f32[2048]{0:T(1024)S(1)} %exponential_reduce_fusion.4), channel_id=25, replica_groups=mesh['pair'=4,'src'=2,'tgt'=4] {'tgt'}, dimensions={0}, use_global_device_ids=true | all-gather | bytes 40960 | tf_op jit(solution)/shard_map/all_gather | solution.py:13
  245.2 4.7 %fusion.13 = f32[1024]{0:T(1024)S(1)} fusion(f32[2048,1024]{0,1:T(8,128)} %copy-done, f32[2048]{0:T(1024)S(1)} %add_multiply_fusion.2, f32[2048]{0:T(1024)S(1)} %fusion.23), kind=kLoop, calls=%fused_computation.71 | loop fusion | flops 8387584 | bytes 8409088 | tf_op jit(solution)/shard_map/reduce_max | solution.py:39
  250.0 5.3 %exponential_reduce_fusion.3 = f32[1024]{0:T(1024)S(1)} fusion(f32[2048,1024]{0,1:T(8,128)} %copy-done, f32[1024]{0:T(1024)S(1)} %fusion.13, f32[2048]{0:T(1024)S(1)} %add_multiply_fusion.2, f32[2048]{0:T(1024)S(1)} %fusion.23), kind=kLoop, calls=%fused_computation.33 | loop fusion | flops 10484736 | bytes 8413184 | tf_op jit(solution)/shard_map/reduce_sum | solution.py:40
  255.3 4.4 all-gather.24
  259.7 4.5 all-gather.25
  267.9 5.2 %all-gather.26 = f32[8192]{0:T(1024)S(1)} all-gather(f32[2048]{0:T(1024)S(1)} %fusion.14), channel_id=28, replica_groups=mesh['pair'=4,'src'=2,'tgt'=4] {'tgt'}, dimensions={0}, use_global_device_ids=true | all-gather | bytes 40960 | tf_op jit(solution)/shard_map/all_gather | solution.py:13
  273.1 5.2 %all-gather.27 = f32[8192]{0:T(1024)S(1)} all-gather(f32[2048]{0:T(1024)S(1)} %exponential_reduce_fusion.2), channel_id=29, replica_groups=mesh['pair'=4,'src'=2,'tgt'=4] {'tgt'}, dimensions={0}, use_global_device_ids=true | all-gather | bytes 40960 | tf_op jit(solution)/shard_map/all_gather | solution.py:13
  278.6 4.7 %fusion.15 = f32[1024]{0:T(1024)S(1)} fusion(f32[2048,1024]{0,1:T(8,128)} %copy-done, f32[2048]{0:T(1024)S(1)} %add_multiply_fusion.1, f32[2048]{0:T(1024)S(1)} %fusion.23), kind=kLoop, calls=%fused_computation.73 | loop fusion | flops 8387584 | bytes 8409088 | tf_op jit(solution)/shard_map/reduce_max | solution.py:39
  283.3 5.3 %exponential_reduce_fusion.1 = f32[1024]{0:T(1024)S(1)} fusion(f32[2048,1024]{0,1:T(8,128)} %copy-done, f32[1024]{0:T(1024)S(1)} %fusion.15, f32[2048]{0:T(1024)S(1)} %add_multiply_fusion.1, f32[2048]{0:T(1024)S(1)} %fusion.23), kind=kLoop, calls=%fused_computation.29 | loop fusion | flops 10484736 | bytes 8413184 | tf_op jit(solution)/shard_map/reduce_sum | solution.py:40
  288.7 4.4 all-gather.28
  293.0 4.3 all-gather.29
  301.1 5.3 %all-gather.30 = f32[8192]{0:T(1024)S(1)} all-gather(f32[2048]{0:T(1024)S(1)} %fusion.16), channel_id=32, replica_groups=mesh['pair'=4,'src'=2,'tgt'=4] {'tgt'}, dimensions={0}, use_global_device_ids=true | all-gather | bytes 40960 | tf_op jit(solution)/shard_map/all_gather | solution.py:13
  306.4 5.2 %all-gather.31 = f32[8192]{0:T(1024)S(1)} all-gather(f32[2048]{0:T(1024)S(1)} %exponential_reduce_fusion), channel_id=33, replica_groups=mesh['pair'=4,'src'=2,'tgt'=4] {'tgt'}, dimensions={0}, use_global_device_ids=true | all-gather | bytes 40960 | tf_op jit(solution)/shard_map/all_gather | solution.py:13
  311.8 4.6 divide_convert_fusion
  320.7 20.0 %reduce-scatter.5.cloned.1.call-done = f32[40,512]{1,0:T(8,128)} async-done(((f32[40,2048]{1,0:T(8,128)}), f32[40,512]{1,0:T(8,128)}) %reduce-scatter.5.cloned.1.call-update) | async-done | bytes 81936 | tf_op jit(solution)/shard_map/reduce_scatter | solution.py:116
  343.1 4.6 collective-permute-done.1
  347.7 9.4 %all_gather.265 = bf16[40,4096]{1,0:T(8,128)(2,1)S(1)} all-gather(bf16[40,512]{1,0:T(8,128)(2,1)S(1)} %collective-permute-done.1), channel_id=1, replica_groups=mesh['pair'=4,'src'=2,'tgt'=4] {'src','tgt'}, dimensions={1}, use_global_device_ids=true | all-gather | bytes 368640 | tf_op jit(solution)/shard_map/all_gather | solution.py:121
  357.1 3.7 fusion.62
  360.9 19.6 %reduce-scatter.7.cloned.1.call-done = f32[40,512]{1,0:T(8,128)} async-done(((f32[40,2048]{1,0:T(8,128)}), f32[40,512]{1,0:T(8,128)}) %reduce-scatter.7.cloned.1.call-update) | async-done | bytes 81936 | tf_op jit(solution)/shard_map/reduce_scatter | solution.py:116
  382.7 4.6 collective-permute-done.2
  387.3 9.6 %all_gather.266 = bf16[40,4096]{1,0:T(8,128)(2,1)S(1)} all-gather(bf16[40,512]{1,0:T(8,128)(2,1)S(1)} %collective-permute-done.2), channel_id=1, replica_groups=mesh['pair'=4,'src'=2,'tgt'=4] {'src','tgt'}, dimensions={1}, use_global_device_ids=true | all-gather | bytes 368640 | tf_op jit(solution)/shard_map/all_gather | solution.py:121
  396.9 3.7 fusion.22
  400.7 19.6 %reduce-scatter.9.cloned.1.call-done = f32[40,512]{1,0:T(8,128)} async-done(((f32[40,2048]{1,0:T(8,128)}), f32[40,512]{1,0:T(8,128)}) %reduce-scatter.9.cloned.1.call-update) | async-done | bytes 81936 | tf_op jit(solution)/shard_map/reduce_scatter | solution.py:116
  422.5 4.6 collective-permute-done.3
  427.1 9.4 %all_gather.267 = bf16[40,4096]{1,0:T(8,128)(2,1)S(1)} all-gather(bf16[40,512]{1,0:T(8,128)(2,1)S(1)} %collective-permute-done.3), channel_id=1, replica_groups=mesh['pair'=4,'src'=2,'tgt'=4] {'src','tgt'}, dimensions={1}, use_global_device_ids=true | all-gather | bytes 368640 | tf_op jit(solution)/shard_map/all_gather | solution.py:121
  436.5 3.7 fusion.17
  440.9 19.1 %reduce-scatter.11.cloned.1.call-done = f32[40,512]{1,0:T(8,128)} async-done(((f32[40,2048]{1,0:T(8,128)}), f32[40,512]{1,0:T(8,128)}) %reduce-scatter.11.cloned.1.call-update) | async-done | bytes 81936 | tf_op jit(solution)/shard_map/reduce_scatter | solution.py:116
  (207 shorter events, 54.9 us)
Async XLA Ops:
  7.2 36.9 %all-reduce.2.cloned.1.call-start = ((), (), s32[]{:S(2)}) async-start(), calls=%async_computation.4 | async-start | bytes 524288 | tf_op jit(solution)/shard_map/psum | solution.py:30
  8.2 11.3 %collective-permute-start = (f32[30,2048]{1,0:T(8,128)S(1)}, f32[30,2048]{1,0:T(8,128)S(1)}, u32[]{:S(2)}, u32[]{:S(2)}) collective-permute-start(f32[30,2048]{1,0:T(8,128)S(1)} %bitcast.139), channel_id=1, source_target_pairs={{8,0},{16,8},{24,16},{9,1},{17,9},{25,17},{10,2},{18,10},{26,18},{... | collective-permute-start | bytes 737288 | tf_op jit(solution)/shard_map/ppermute | solution.py:25
  20.2 320.5 %reduce-scatter.5.cloned.1.call-start = ((), (), s32[]{:S(2)}) async-start(), calls=%async_computation.5 | async-start | bytes 409600 | tf_op jit(solution)/shard_map/reduce_scatter | solution.py:116
  55.0 12.8 %copy-start = (f32[2048,1024]{0,1:T(8,128)}, f32[2048,1024]{0,1:T(8,128)S(1)}, u32[]{:S(2)}) copy-start(f32[2048,1024]{0,1:T(8,128)S(1)} %get-tuple-element.1373) | copy-start | bytes 25165828
  80.7 5.8 %copy-start.1 = (f32[2048,1024]{0,1:T(8,128)S(1)}, f32[2048,1024]{0,1:T(8,128)}, u32[]{:S(2)}) copy-start(f32[2048,1024]{0,1:T(8,128)} %copy-done) | copy-start | bytes 25165828
  111.9 19.1 %slice-start = ((s8[8388608]{0:T(1024)(128)(4,1)}), s8[4194304]{0:T(1024)(128)(4,1)S(1)}, s32[]{:S(2)}) async-start(s8[8388608]{0:T(1024)(128)(4,1)} %bitcast.111), calls=%async_computation.9 | async-start | bytes 8388608
  116.7 14.3 %slice-start.1 = ((s8[8388608]{0:T(1024)(128)(4,1)}), s8[4194304]{0:T(1024)(128)(4,1)S(1)}, s32[]{:S(2)}) async-start(s8[8388608]{0:T(1024)(128)(4,1)} %bitcast.111), calls=%async_computation.10 | async-start | bytes 8388608
  145.3 18.9 %slice-start.2 = ((s8[8388608]{0:T(1024)(128)(4,1)}), s8[4194304]{0:T(1024)(128)(4,1)S(1)}, s32[]{:S(2)}) async-start(s8[8388608]{0:T(1024)(128)(4,1)} %bitcast.113), calls=%async_computation.11 | async-start | bytes 8388608
  150.1 14.1 %slice-start.3 = ((s8[8388608]{0:T(1024)(128)(4,1)}), s8[4194304]{0:T(1024)(128)(4,1)S(1)}, s32[]{:S(2)}) async-start(s8[8388608]{0:T(1024)(128)(4,1)} %bitcast.113), calls=%async_computation.12 | async-start | bytes 8388608
  178.5 19.3 %slice-start.4 = ((s8[8388608]{0:T(1024)(128)(4,1)}), s8[4194304]{0:T(1024)(128)(4,1)S(1)}, s32[]{:S(2)}) async-start(s8[8388608]{0:T(1024)(128)(4,1)} %bitcast.115), calls=%async_computation.13 | async-start | bytes 8388608
  183.2 14.5 %slice-start.5 = ((s8[8388608]{0:T(1024)(128)(4,1)}), s8[4194304]{0:T(1024)(128)(4,1)S(1)}, s32[]{:S(2)}) async-start(s8[8388608]{0:T(1024)(128)(4,1)} %bitcast.115), calls=%async_computation.14 | async-start | bytes 8388608
  212.1 18.9 %slice-start.6 = ((s8[8388608]{0:T(1024)(128)(4,1)}), s8[4194304]{0:T(1024)(128)(4,1)S(1)}, s32[]{:S(2)}) async-start(s8[8388608]{0:T(1024)(128)(4,1)} %bitcast.117), calls=%async_computation.15 | async-start | bytes 8388608
  216.8 14.1 %slice-start.7 = ((s8[8388608]{0:T(1024)(128)(4,1)}), s8[4194304]{0:T(1024)(128)(4,1)S(1)}, s32[]{:S(2)}) async-start(s8[8388608]{0:T(1024)(128)(4,1)} %bitcast.117), calls=%async_computation.16 | async-start | bytes 8388608
  245.2 19.0 %slice-start.8 = ((s8[8388608]{0:T(1024)(128)(4,1)}), s8[4194304]{0:T(1024)(128)(4,1)S(1)}, s32[]{:S(2)}) async-start(s8[8388608]{0:T(1024)(128)(4,1)} %bitcast.119), calls=%async_computation.17 | async-start | bytes 8388608
  250.0 14.3 %slice-start.9 = ((s8[8388608]{0:T(1024)(128)(4,1)}), s8[4194304]{0:T(1024)(128)(4,1)S(1)}, s32[]{:S(2)}) async-start(s8[8388608]{0:T(1024)(128)(4,1)} %bitcast.119), calls=%async_computation.18 | async-start | bytes 8388608
  278.6 18.9 %slice-start.10 = ((s8[8388608]{0:T(1024)(128)(4,1)}), s8[4194304]{0:T(1024)(128)(4,1)S(1)}, s32[]{:S(2)}) async-start(s8[8388608]{0:T(1024)(128)(4,1)} %bitcast.121), calls=%async_computation.19 | async-start | bytes 8388608
  283.3 14.1 %slice-start.11 = ((s8[8388608]{0:T(1024)(128)(4,1)}), s8[4194304]{0:T(1024)(128)(4,1)S(1)}, s32[]{:S(2)}) async-start(s8[8388608]{0:T(1024)(128)(4,1)} %bitcast.121), calls=%async_computation.20 | async-start | bytes 8388608
  301.1 17.3 %copy-start.3 = (f32[40,1024]{1,0:T(8,128)S(1)}, f32[40,1024]{1,0:T(8,128)}, u32[]{:S(2)}) copy-start(f32[40,1024]{1,0:T(8,128)} %param.25) | copy-start | bytes 491524
  316.5 1.9 copy-start.2
  320.0 60.5 %reduce-scatter.7.cloned.1.call-start = ((), (), s32[]{:S(2)}) async-start(), calls=%async_computation.6 | async-start | bytes 409600 | tf_op jit(solution)/shard_map/reduce_scatter | solution.py:116
  341.6 118.3 %copy-start.4 = (f32[40,512]{1,0:T(8,128)S(1)}, f32[40,512]{1,0:T(8,128)}, u32[]{:S(2)}) copy-start(f32[40,512]{1,0:T(8,128)} %reduce-scatter.5.cloned.1.call-done) | copy-start | bytes 245764
  341.6 6.0 %collective-permute-start.1 = (bf16[40,512]{1,0:T(8,128)(2,1)S(1)}, bf16[40,512]{1,0:T(8,128)(2,1)S(1)}, u32[]{:S(2)}, u32[]{:S(2)}) collective-permute-start(bf16[40,512]{1,0:T(8,128)(2,1)S(1)} %select_convert_fusion.2), channel_id=1, source_target_pairs={{8,0},{16,8},{24,16},{9,1},{17,9},{25,17},{10,2},{18,10},{26,18},{... | collective-permute-start | bytes 122888 | tf_op jit(solution)/shard_map/ppermute | solution.py:25
  360.8 59.5 %reduce-scatter.9.cloned.1.call-start = ((), (), s32[]{:S(2)}) async-start(), calls=%async_computation.7 | async-start | bytes 409600 | tf_op jit(solution)/shard_map/reduce_scatter | solution.py:116
  380.4 79.5 %copy-start.5 = (f32[40,512]{1,0:T(8,128)S(1)}, f32[40,512]{1,0:T(8,128)}, u32[]{:S(2)}) copy-start(f32[40,512]{1,0:T(8,128)} %reduce-scatter.7.cloned.1.call-done) | copy-start | bytes 245764
  381.4 5.9 %collective-permute-start.2 = (bf16[40,512]{1,0:T(8,128)(2,1)S(1)}, bf16[40,512]{1,0:T(8,128)(2,1)S(1)}, u32[]{:S(2)}, u32[]{:S(2)}) collective-permute-start(bf16[40,512]{1,0:T(8,128)(2,1)S(1)} %select_convert_fusion.1), channel_id=1, source_target_pairs={{8,0},{16,8},{24,16},{9,1},{17,9},{25,17},{10,2},{18,10},{26,18},{... | collective-permute-start | bytes 122888 | tf_op jit(solution)/shard_map/ppermute | solution.py:25
  400.7 59.2 %reduce-scatter.11.cloned.1.call-start = ((), (), s32[]{:S(2)}) async-start(), calls=%async_computation.8 | async-start | bytes 409600 | tf_op jit(solution)/shard_map/reduce_scatter | solution.py:116
  421.2 5.9 %collective-permute-start.3 = (bf16[40,512]{1,0:T(8,128)(2,1)S(1)}, bf16[40,512]{1,0:T(8,128)(2,1)S(1)}, u32[]{:S(2)}, u32[]{:S(2)}) collective-permute-start(bf16[40,512]{1,0:T(8,128)(2,1)S(1)} %select_convert_fusion), channel_id=1, source_target_pairs={{8,0},{16,8},{24,16},{9,1},{17,9},{25,17},{10,2},{18,10},{26,18},{... | collective-permute-start | bytes 122888 | tf_op jit(solution)/shard_map/ppermute | solution.py:25
Sparse Core Ops, SparseCore 0:
  20.4 23.6 all-reduce.1
  320.1 20.5 reduce-scatter.4
  361.0 19.4 reduce-scatter.6
  400.8 19.4 reduce-scatter.8
  440.4 19.4 reduce-scatter.10
where the time goes:
time: 477 us; the launch traced here: 468 us
  blocking collectives  182 us (38%)
  waiting for transfers between devices  120 us (25%)
  other arithmetic  115 us (24%)
  matrix products  22.8 us (5%)
  between operations  16.2 us (3%)
  local copies, waits for them, and re-layouts  6.12 us (1%)
  starting transfers between devices  5.5 us (1%)
    all_gather x32, blocking collectives, joined(): everything = jax.tree.map(lambda part: lax.all_gather(part, axis), shard)  154 us
    reduce_scatter x4, waiting for transfers between devices, local(): lax.psum_scatter(partial_value, 'tgt', scatter_dimension=1, tiled=True)  78.2 us
    reduce_sum x8, other arithmetic, column_lse(): totals = jnp.sum(jnp.exp(col_scores - peak[None, :]), axis=0)  37 us
    reduce_max x7, other arithmetic, column_lse(): peak = jnp.max(col_scores, axis=0)  33.1 us
    all_gather x3, blocking collectives, local(): gathered = lax.all_gather(passed, ('src', 'tgt'), axis=1, tiled=True)  28.4 us
    psum x1, waiting for transfers between devices, from_root(): return lax.psum(jnp.where(mine, shard, jnp.zeros_like(shard)), axis)  22.5 us
    ppermute x4, waiting for transfers between devices, shifted(): return lax.ppermute(shard, axis, pairs)  19.2 us
    reduce_sum x8, other arithmetic, row_lse(): totals = jnp.sum(jnp.exp(row_scores - peak[:, None]), axis=1)  17.8 us
  transfers between devices with their start and end apart: 9, of which 9 were waited for; matrix products, arithmetic and copies ran while one was open for 1% of the time, Pallas kernels for 0%

commit v1 on v0

--- a/solution.py
+++ b/solution.py
@@ -7,6 +7,7 @@
 EPS = 0.1
 LAM = 1.0
 NEG = -1e30
+remake_block = lambda x0, axis_id: jnp.sum(jax.lax.all_gather(x0, axis_id), axis=0)
 
 
 def joined(shard, axis, combine):
@@ -27,7 +28,7 @@
 
 def from_root(shard, axis, root):
     mine = lax.axis_index(axis) == root
-    return lax.psum(jnp.where(mine, shard, jnp.zeros_like(shard)), axis)
+    return remake_block(jnp.where(mine, shard, jnp.zeros_like(shard)), axis)
 
 
 def combine(first, second):

time: 477 us -> 461 us (0.966)
  waiting for transfers between devices: 120 us -> 97 us
  blocking collectives: 182 us -> 190 us
    psum x1 -> x0, waiting for transfers between devices: 22.5 us -> none  [from_root(): return lax.psum(jnp.where(mine, shard, jnp.zeros_like(shard)), axis)]
    all_gather x0 -> x1, blocking collectives: none -> 8.13 us  [jax.lax.all_gather(x0, axis_id)]
  transfers between devices with their start and end apart: 9 -> 8, of which waited for: 9 -> 8; matrix products, arithmetic and copies ran while one was open for 1% -> 1% of each run, Pallas kernels for 0% -> 0%
where the time goes in v1:
time: 461 us; the launch traced here: 452 us
  blocking collectives  190 us (41%)
  other arithmetic  113 us (25%)
  waiting for transfers between devices  97 us (21%)
  matrix products  22.7 us (5%)
  between operations  16.2 us (4%)
  local copies, waits for them, and re-layouts  6.11 us (1%)
  starting transfers between devices  5.45 us (1%)
    all_gather x32, blocking collectives, joined(): everything = jax.tree.map(lambda part: lax.all_gather(part, axis), shard)  154 us
    reduce_scatter x4, waiting for transfers between devices, local(): lax.psum_scatter(partial_value, 'tgt', scatter_dimension=1, tiled=True)  79 us
    reduce_sum x8, other arithmetic, column_lse(): totals = jnp.sum(jnp.exp(col_scores - peak[None, :]), axis=0)  37 us
    reduce_max x7, other arithmetic, column_lse(): peak = jnp.max(col_scores, axis=0)  33.2 us
    all_gather x3, blocking collectives, local(): gathered = lax.all_gather(passed, ('src', 'tgt'), axis=1, tiled=True)  28.4 us
    ppermute x4, waiting for transfers between devices, shifted(): return lax.ppermute(shard, axis, pairs)  17.9 us
    reduce_sum x8, other arithmetic, row_lse(): totals = jnp.sum(jnp.exp(row_scores - peak[:, None]), axis=1)  17.9 us
    dot_general x4, matrix products, local(): lax.dot_general(handed, weights, (((1,), (1,)), ((), ())), preferred_elem...  12.8 us
  transfers between devices with their start and end apart: 8, of which 8 were waited for; matrix products, arithmetic and copies ran while one was open for 1% of the time, Pallas kernels for 0%

profile of v1, /device:TPU:0, one launch (start us, length us, event | category | flops | bytes accessed | tf_op | source)
XLA Modules:
  0.0 451.9 jit_solution(15774652557234006693)
XLA Ops:
  15.4 4.1 collective-permute-done
  19.5 8.1 %all-gather.33 = f32[2,30,2048]{2,1,0:T(8,128)S(1)} all-gather(f32[1,30,2048]{2,1,0:T(8,128)S(1)} %select_bitcast_fusion), channel_id=2, replica_groups=mesh['pair'=4,'src'=2,'tgt'=4] {'src'}, dimensions={0}, use_global_device_ids=true | all-gather | bytes 737280 | tf_op jit(solution)/shard_map/all_gather | solution.py:10
  27.7 9.9 %fusion.1 = (f32[1024]{0:T(1024)S(1)}, f32[2048,1024]{0,1:T(8,128)S(1)}) fusion(f32[2048]{0:T(1024)S(1)} %fusion.23, f32[1,30,2048]{2,0,1:T(1,128)} %param.21, f32[30,1024]{1,0:T(8,128)} %param.22, f32[30,2048]{1,0:T(8,128)S(1)} %reduce_sum.172, s32[]{:T(128)S(6)} %select_n.247, pred[]{:T(512)S(6)} %eq.24, f32[1024]{0:T(1024)S(1)} %multiply_reduce_fusion.1, ...), kind=kOutput, calls=%fused_computation.59 | convolution fusion | flops 771781632 | bytes 8912901 | tf_op jit(solution)/shard_map/dot_general | solution.py:72
  37.7 4.4 all-gather.1
  42.0 2.5 exponential_reduce_fusion.15
  44.5 4.5 %all-gather.2 = f32[2048]{0:T(1024)S(1)} all-gather(f32[1024]{0:T(1024)S(1)} %exponential_reduce_fusion.15), channel_id=4, replica_groups=mesh['pair'=4,'src'=2,'tgt'=4] {'src'}, dimensions={0}, use_global_device_ids=true | all-gather | bytes 12288 | tf_op jit(solution)/shard_map/all_gather | solution.py:14
  52.7 5.2 %all-gather.3 = f32[8192]{0:T(1024)S(1)} all-gather(f32[2048]{0:T(1024)S(1)} %fusion.2), channel_id=5, replica_groups=mesh['pair'=4,'src'=2,'tgt'=4] {'tgt'}, dimensions={0}, use_global_device_ids=true | all-gather | bytes 40960 | tf_op jit(solution)/shard_map/all_gather | solution.py:14
  57.9 5.2 %all-gather.4 = f32[8192]{0:T(1024)S(1)} all-gather(f32[2048]{0:T(1024)S(1)} %exponential_reduce_fusion.14), channel_id=6, replica_groups=mesh['pair'=4,'src'=2,'tgt'=4] {'tgt'}, dimensions={0}, use_global_device_ids=true | all-gather | bytes 40960 | tf_op jit(solution)/shard_map/all_gather | solution.py:14
  63.4 4.7 %fusion.3 = f32[1024]{0:T(1024)S(1)} fusion(f32[2048,1024]{0,1:T(8,128)} %copy-done, f32[2048]{0:T(1024)S(1)} %add_multiply_fusion.7, f32[2048]{0:T(1024)S(1)} %fusion.23), kind=kLoop, calls=%fused_computation.61 | loop fusion | flops 8387584 | bytes 8409088 | tf_op jit(solution)/shard_map/reduce_max | solution.py:40
  69.1 2.5 exponential_reduce_fusion.13
  71.6 4.4 all-gather.5
  76.0 4.3 all-gather.6
  84.0 5.2 %all-gather.7 = f32[8192]{0:T(1024)S(1)} all-gather(f32[2048]{0:T(1024)S(1)} %fusion.4), channel_id=9, replica_groups=mesh['pair'=4,'src'=2,'tgt'=4] {'tgt'}, dimensions={0}, use_global_device_ids=true | all-gather | bytes 40960 | tf_op jit(solution)/shard_map/all_gather | solution.py:14
  89.2 5.2 %all-gather.8 = f32[8192]{0:T(1024)S(1)} all-gather(f32[2048]{0:T(1024)S(1)} %exponential_reduce_fusion.12), channel_id=10, replica_groups=mesh['pair'=4,'src'=2,'tgt'=4] {'tgt'}, dimensions={0}, use_global_device_ids=true | all-gather | bytes 40960 | tf_op jit(solution)/shard_map/all_gather | solution.py:14
  94.6 4.7 %fusion.5 = f32[1024]{0:T(1024)S(1)} fusion(f32[2048,1024]{0,1:T(8,128)} %copy-done, f32[2048]{0:T(1024)S(1)} %add_multiply_fusion.6, f32[2048]{0:T(1024)S(1)} %fusion.23), kind=kLoop, calls=%fused_computation.63 | loop fusion | flops 8387584 | bytes 8409088 | tf_op jit(solution)/shard_map/reduce_max | solution.py:40
  99.4 5.3 %exponential_reduce_fusion.11 = f32[1024]{0:T(1024)S(1)} fusion(f32[2048,1024]{0,1:T(8,128)} %copy-done, f32[1024]{0:T(1024)S(1)} %fusion.5, f32[2048]{0:T(1024)S(1)} %add_multiply_fusion.6, f32[2048]{0:T(1024)S(1)} %fusion.23), kind=kLoop, calls=%fused_computation.49 | loop fusion | flops 10484736 | bytes 8413184 | tf_op jit(solution)/shard_map/reduce_sum | solution.py:41
  104.7 4.4 all-gather.9
  109.1 4.6 %all-gather.10 = f32[2048]{0:T(1024)S(1)} all-gather(f32[1024]{0:T(1024)S(1)} %exponential_reduce_fusion.11), channel_id=12, replica_groups=mesh['pair'=4,'src'=2,'tgt'=4] {'src'}, dimensions={0}, use_global_device_ids=true | all-gather | bytes 12288 | tf_op jit(solution)/shard_map/all_gather | solution.py:14
  117.4 5.2 %all-gather.11 = f32[8192]{0:T(1024)S(1)} all-gather(f32[2048]{0:T(1024)S(1)} %fusion.6), channel_id=13, replica_groups=mesh['pair'=4,'src'=2,'tgt'=4] {'tgt'}, dimensions={0}, use_global_device_ids=true | all-gather | bytes 40960 | tf_op jit(solution)/shard_map/all_gather | solution.py:14
  122.6 5.2 %all-gather.12 = f32[8192]{0:T(1024)S(1)} all-gather(f32[2048]{0:T(1024)S(1)} %exponential_reduce_fusion.10), channel_id=14, replica_groups=mesh['pair'=4,'src'=2,'tgt'=4] {'tgt'}, dimensions={0}, use_global_device_ids=true | all-gather | bytes 40960 | tf_op jit(solution)/shard_map/all_gather | solution.py:14
  128.0 4.7 %fusion.7 = f32[1024]{0:T(1024)S(1)} fusion(f32[2048,1024]{0,1:T(8,128)} %copy-done, f32[2048]{0:T(1024)S(1)} %add_multiply_fusion.5, f32[2048]{0:T(1024)S(1)} %fusion.23), kind=kLoop, calls=%fused_computation.65 | loop fusion | flops 8387584 | bytes 8409088 | tf_op jit(solution)/shard_map/reduce_max | solution.py:40
  132.8 5.3 %exponential_reduce_fusion.9 = f32[1024]{0:T(1024)S(1)} fusion(f32[2048,1024]{0,1:T(8,128)} %copy-done, f32[1024]{0:T(1024)S(1)} %fusion.7, f32[2048]{0:T(1024)S(1)} %add_multiply_fusion.5, f32[2048]{0:T(1024)S(1)} %fusion.23), kind=kLoop, calls=%fused_computation.45 | loop fusion | flops 10484736 | bytes 8413184 | tf_op jit(solution)/shard_map/reduce_sum | solution.py:41
  138.1 4.4 all-gather.13
  142.5 4.3 all-gather.14
  150.6 5.2 %all-gather.15 = f32[8192]{0:T(1024)S(1)} all-gather(f32[2048]{0:T(1024)S(1)} %fusion.8), channel_id=17, replica_groups=mesh['pair'=4,'src'=2,'tgt'=4] {'tgt'}, dimensions={0}, use_global_device_ids=true | all-gather | bytes 40960 | tf_op jit(solution)/shard_map/all_gather | solution.py:14
  155.8 5.2 %all-gather.16 = f32[8192]{0:T(1024)S(1)} all-gather(f32[2048]{0:T(1024)S(1)} %exponential_reduce_fusion.8), channel_id=18, replica_groups=mesh['pair'=4,'src'=2,'tgt'=4] {'tgt'}, dimensions={0}, use_global_device_ids=true | all-gather | bytes 40960 | tf_op jit(solution)/shard_map/all_gather | solution.py:14
  161.2 4.7 %fusion.9 = f32[1024]{0:T(1024)S(1)} fusion(f32[2048,1024]{0,1:T(8,128)} %copy-done, f32[2048]{0:T(1024)S(1)} %add_multiply_fusion.4, f32[2048]{0:T(1024)S(1)} %fusion.23), kind=kLoop, calls=%fused_computation.67 | loop fusion | flops 8387584 | bytes 8409088 | tf_op jit(solution)/shard_map/reduce_max | solution.py:40
  166.0 5.3 %exponential_reduce_fusion.7 = f32[1024]{0:T(1024)S(1)} fusion(f32[2048,1024]{0,1:T(8,128)} %copy-done, f32[1024]{0:T(1024)S(1)} %fusion.9, f32[2048]{0:T(1024)S(1)} %add_multiply_fusion.4, f32[2048]{0:T(1024)S(1)} %fusion.23), kind=kLoop, calls=%fused_computation.41 | loop fusion | flops 10484736 | bytes 8413184 | tf_op jit(solution)/shard_map/reduce_sum | solution.py:41
  171.3 4.4 all-gather.17
  175.7 4.8 %all-gather.18 = f32[2048]{0:T(1024)S(1)} all-gather(f32[1024]{0:T(1024)S(1)} %exponential_reduce_fusion.7), channel_id=20, replica_groups=mesh['pair'=4,'src'=2,'tgt'=4] {'src'}, dimensions={0}, use_global_device_ids=true | all-gather | bytes 12288 | tf_op jit(solution)/shard_map/all_gather | solution.py:14
  184.2 5.2 %all-gather.19 = f32[8192]{0:T(1024)S(1)} all-gather(f32[2048]{0:T(1024)S(1)} %fusion.10), channel_id=21, replica_groups=mesh['pair'=4,'src'=2,'tgt'=4] {'tgt'}, dimensions={0}, use_global_device_ids=true | all-gather | bytes 40960 | tf_op jit(solution)/shard_map/all_gather | solution.py:14
  189.4 5.2 %all-gather.20 = f32[8192]{0:T(1024)S(1)} all-gather(f32[2048]{0:T(1024)S(1)} %exponential_reduce_fusion.6), channel_id=22, replica_groups=mesh['pair'=4,'src'=2,'tgt'=4] {'tgt'}, dimensions={0}, use_global_device_ids=true | all-gather | bytes 40960 | tf_op jit(solution)/shard_map/all_gather | solution.py:14
  194.8 4.7 %fusion.11 = f32[1024]{0:T(1024)S(1)} fusion(f32[2048,1024]{0,1:T(8,128)} %copy-done, f32[2048]{0:T(1024)S(1)} %add_multiply_fusion.3, f32[2048]{0:T(1024)S(1)} %fusion.23), kind=kLoop, calls=%fused_computation.69 | loop fusion | flops 8387584 | bytes 8409088 | tf_op jit(solution)/shard_map/reduce_max | solution.py:40
  199.6 5.3 %exponential_reduce_fusion.5 = f32[1024]{0:T(1024)S(1)} fusion(f32[2048,1024]{0,1:T(8,128)} %copy-done, f32[1024]{0:T(1024)S(1)} %fusion.11, f32[2048]{0:T(1024)S(1)} %add_multiply_fusion.3, f32[2048]{0:T(1024)S(1)} %fusion.23), kind=kLoop, calls=%fused_computation.37 | loop fusion | flops 10484736 | bytes 8413184 | tf_op jit(solution)/shard_map/reduce_sum | solution.py:41
  204.9 4.4 all-gather.21
  209.3 4.3 all-gather.22
  217.4 5.2 %all-gather.23 = f32[8192]{0:T(1024)S(1)} all-gather(f32[2048]{0:T(1024)S(1)} %fusion.12), channel_id=25, replica_groups=mesh['pair'=4,'src'=2,'tgt'=4] {'tgt'}, dimensions={0}, use_global_device_ids=true | all-gather | bytes 40960 | tf_op jit(solution)/shard_map/all_gather | solution.py:14
  222.6 5.2 %all-gather.24 = f32[8192]{0:T(1024)S(1)} all-gather(f32[2048]{0:T(1024)S(1)} %exponential_reduce_fusion.4), channel_id=26, replica_groups=mesh['pair'=4,'src'=2,'tgt'=4] {'tgt'}, dimensions={0}, use_global_device_ids=true | all-gather | bytes 40960 | tf_op jit(solution)/shard_map/all_gather | solution.py:14
  228.0 4.7 %fusion.13 = f32[1024]{0:T(1024)S(1)} fusion(f32[2048,1024]{0,1:T(8,128)} %copy-done, f32[2048]{0:T(1024)S(1)} %add_multiply_fusion.2, f32[2048]{0:T(1024)S(1)} %fusion.23), kind=kLoop, calls=%fused_computation.71 | loop fusion | flops 8387584 | bytes 8409088 | tf_op jit(solution)/shard_map/reduce_max | solution.py:40
  232.8 5.3 %exponential_reduce_fusion.3 = f32[1024]{0:T(1024)S(1)} fusion(f32[2048,1024]{0,1:T(8,128)} %copy-done, f32[1024]{0:T(1024)S(1)} %fusion.13, f32[2048]{0:T(1024)S(1)} %add_multiply_fusion.2, f32[2048]{0:T(1024)S(1)} %fusion.23), kind=kLoop, calls=%fused_computation.33 | loop fusion | flops 10484736 | bytes 8413184 | tf_op jit(solution)/shard_map/reduce_sum | solution.py:41
  238.1 4.4 all-gather.25
  242.5 4.5 %all-gather.26 = f32[2048]{0:T(1024)S(1)} all-gather(f32[1024]{0:T(1024)S(1)} %exponential_reduce_fusion.3), channel_id=28, replica_groups=mesh['pair'=4,'src'=2,'tgt'=4] {'src'}, dimensions={0}, use_global_device_ids=true | all-gather | bytes 12288 | tf_op jit(solution)/shard_map/all_gather | solution.py:14
  250.7 5.2 %all-gather.27 = f32[8192]{0:T(1024)S(1)} all-gather(f32[2048]{0:T(1024)S(1)} %fusion.14), channel_id=29, replica_groups=mesh['pair'=4,'src'=2,'tgt'=4] {'tgt'}, dimensions={0}, use_global_device_ids=true | all-gather | bytes 40960 | tf_op jit(solution)/shard_map/all_gather | solution.py:14
  255.9 5.2 %all-gather.28 = f32[8192]{0:T(1024)S(1)} all-gather(f32[2048]{0:T(1024)S(1)} %exponential_reduce_fusion.2), channel_id=30, replica_groups=mesh['pair'=4,'src'=2,'tgt'=4] {'tgt'}, dimensions={0}, use_global_device_ids=true | all-gather | bytes 40960 | tf_op jit(solution)/shard_map/all_gather | solution.py:14
  261.4 4.7 %fusion.15 = f32[1024]{0:T(1024)S(1)} fusion(f32[2048,1024]{0,1:T(8,128)} %copy-done, f32[2048]{0:T(1024)S(1)} %add_multiply_fusion.1, f32[2048]{0:T(1024)S(1)} %fusion.23), kind=kLoop, calls=%fused_computation.73 | loop fusion | flops 8387584 | bytes 8409088 | tf_op jit(solution)/shard_map/reduce_max | solution.py:40
  266.1 5.3 %exponential_reduce_fusion.1 = f32[1024]{0:T(1024)S(1)} fusion(f32[2048,1024]{0,1:T(8,128)} %copy-done, f32[1024]{0:T(1024)S(1)} %fusion.15, f32[2048]{0:T(1024)S(1)} %add_multiply_fusion.1, f32[2048]{0:T(1024)S(1)} %fusion.23), kind=kLoop, calls=%fused_computation.29 | loop fusion | flops 10484736 | bytes 8413184 | tf_op jit(solution)/shard_map/reduce_sum | solution.py:41
  271.5 4.4 all-gather.29
  275.8 4.3 all-gather.30
  283.9 5.3 %all-gather.31 = f32[8192]{0:T(1024)S(1)} all-gather(f32[2048]{0:T(1024)S(1)} %fusion.16), channel_id=33, replica_groups=mesh['pair'=4,'src'=2,'tgt'=4] {'tgt'}, dimensions={0}, use_global_device_ids=true | all-gather | bytes 40960 | tf_op jit(solution)/shard_map/all_gather | solution.py:14
  289.2 5.2 %all-gather.32 = f32[8192]{0:T(1024)S(1)} all-gather(f32[2048]{0:T(1024)S(1)} %exponential_reduce_fusion), channel_id=34, replica_groups=mesh['pair'=4,'src'=2,'tgt'=4] {'tgt'}, dimensions={0}, use_global_device_ids=true | all-gather | bytes 40960 | tf_op jit(solution)/shard_map/all_gather | solution.py:14
  294.7 4.6 %divide_convert_fusion = bf16[2048,1024]{0,1:T(8,128)(2,1)S(1)} fusion(f32[2048,1024]{0,1:T(8,128)} %copy-done, f32[2048]{0:T(1024)S(1)} %get-tuple-element.1225, f32[2048]{0:T(1024)S(1)} %get-tuple-element.1224, f32[1024]{0:T(1024)S(1)} %bitcast.144, f32[1024]{0:T(1024)S(1)} %fusion.40), kind=kLoop, calls=%fused_computation.26 | loop fusion | flops 12582912 | bytes 12607488 | tf_op jit(solution)/shard_map/convert_element_type | solution.py:107
  303.5 20.8 %reduce-scatter.5.cloned.1.call-done = f32[40,512]{1,0:T(8,128)} async-done(((f32[40,2048]{1,0:T(8,128)}), f32[40,512]{1,0:T(8,128)}) %reduce-scatter.5.cloned.1.call-update) | async-done | bytes 81936 | tf_op jit(solution)/shard_map/reduce_scatter | solution.py:117
  326.7 4.6 %collective-permute-done.1 = bf16[40,512]{1,0:T(8,128)(2,1)S(1)} collective-permute-done((bf16[40,512]{1,0:T(8,128)(2,1)S(1)}, bf16[40,512]{1,0:T(8,128)(2,1)S(1)}, u32[]{:S(2)}, u32[]{:S(2)}) %collective-permute-start.1) | collective-permute-done | bytes 40992 | tf_op jit(solution)/shard_map/ppermute | solution.py:26
  331.2 9.4 %all_gather.273 = bf16[40,4096]{1,0:T(8,128)(2,1)S(1)} all-gather(bf16[40,512]{1,0:T(8,128)(2,1)S(1)} %collective-permute-done.1), channel_id=1, replica_groups=mesh['pair'=4,'src'=2,'tgt'=4] {'src','tgt'}, dimensions={1}, use_global_device_ids=true | all-gather | bytes 368640 | tf_op jit(solution)/shard_map/all_gather | solution.py:122
  340.7 3.7 fusion.62
  344.5 19.6 %reduce-scatter.7.cloned.1.call-done = f32[40,512]{1,0:T(8,128)} async-done(((f32[40,2048]{1,0:T(8,128)}), f32[40,512]{1,0:T(8,128)}) %reduce-scatter.7.cloned.1.call-update) | async-done | bytes 81936 | tf_op jit(solution)/shard_map/reduce_scatter | solution.py:117
  366.4 4.6 %collective-permute-done.2 = bf16[40,512]{1,0:T(8,128)(2,1)S(1)} collective-permute-done((bf16[40,512]{1,0:T(8,128)(2,1)S(1)}, bf16[40,512]{1,0:T(8,128)(2,1)S(1)}, u32[]{:S(2)}, u32[]{:S(2)}) %collective-permute-start.2) | collective-permute-done | bytes 40992 | tf_op jit(solution)/shard_map/ppermute | solution.py:26
  370.9 9.6 %all_gather.274 = bf16[40,4096]{1,0:T(8,128)(2,1)S(1)} all-gather(bf16[40,512]{1,0:T(8,128)(2,1)S(1)} %collective-permute-done.2), channel_id=1, replica_groups=mesh['pair'=4,'src'=2,'tgt'=4] {'src','tgt'}, dimensions={1}, use_global_device_ids=true | all-gather | bytes 368640 | tf_op jit(solution)/shard_map/all_gather | solution.py:122
  380.5 3.7 fusion.22
  384.4 19.6 %reduce-scatter.9.cloned.1.call-done = f32[40,512]{1,0:T(8,128)} async-done(((f32[40,2048]{1,0:T(8,128)}), f32[40,512]{1,0:T(8,128)}) %reduce-scatter.9.cloned.1.call-update) | async-done | bytes 81936 | tf_op jit(solution)/shard_map/reduce_scatter | solution.py:117
  406.1 4.6 %collective-permute-done.3 = bf16[40,512]{1,0:T(8,128)(2,1)S(1)} collective-permute-done((bf16[40,512]{1,0:T(8,128)(2,1)S(1)}, bf16[40,512]{1,0:T(8,128)(2,1)S(1)}, u32[]{:S(2)}, u32[]{:S(2)}) %collective-permute-start.3) | collective-permute-done | bytes 40992 | tf_op jit(solution)/shard_map/ppermute | solution.py:26
  410.7 9.4 %all_gather.275 = bf16[40,4096]{1,0:T(8,128)(2,1)S(1)} all-gather(bf16[40,512]{1,0:T(8,128)(2,1)S(1)} %collective-permute-done.3), channel_id=1, replica_groups=mesh['pair'=4,'src'=2,'tgt'=4] {'src','tgt'}, dimensions={1}, use_global_device_ids=true | all-gather | bytes 368640 | tf_op jit(solution)/shard_map/all_gather | solution.py:122
  420.1 3.7 fusion.17
  424.5 19.1 %reduce-scatter.11.cloned.1.call-done = f32[40,512]{1,0:T(8,128)} async-done(((f32[40,2048]{1,0:T(8,128)}), f32[40,512]{1,0:T(8,128)}) %reduce-scatter.11.cloned.1.call-update) | async-done | bytes 81936 | tf_op jit(solution)/shard_map/reduce_scatter | solution.py:117
  (206 shorter events, 53.3 us)
Async XLA Ops:
  7.2 317.2 %reduce-scatter.5.cloned.1.call-start = ((), (), s32[]{:S(2)}) async-start(), calls=%async_computation.4 | async-start | bytes 409600 | tf_op jit(solution)/shard_map/reduce_scatter | solution.py:117
  8.2 11.3 %collective-permute-start = (f32[30,2048]{1,0:T(8,128)S(1)}, f32[30,2048]{1,0:T(8,128)S(1)}, u32[]{:S(2)}, u32[]{:S(2)}) collective-permute-start(f32[30,2048]{1,0:T(8,128)S(1)} %bitcast.141), channel_id=1, source_target_pairs={{8,0},{16,8},{24,16},{9,1},{17,9},{25,17},{10,2},{18,10},{26,18},{... | collective-permute-start | bytes 737288 | tf_op jit(solution)/shard_map/ppermute | solution.py:26
  37.6 12.8 %copy-start = (f32[2048,1024]{0,1:T(8,128)}, f32[2048,1024]{0,1:T(8,128)S(1)}, u32[]{:S(2)}) copy-start(f32[2048,1024]{0,1:T(8,128)S(1)} %get-tuple-element.1373) | copy-start | bytes 25165828
  63.4 5.8 %copy-start.1 = (f32[2048,1024]{0,1:T(8,128)S(1)}, f32[2048,1024]{0,1:T(8,128)}, u32[]{:S(2)}) copy-start(f32[2048,1024]{0,1:T(8,128)} %copy-done) | copy-start | bytes 25165828
  94.6 19.1 %slice-start = ((s8[8388608]{0:T(1024)(128)(4,1)}), s8[4194304]{0:T(1024)(128)(4,1)S(1)}, s32[]{:S(2)}) async-start(s8[8388608]{0:T(1024)(128)(4,1)} %bitcast.113), calls=%async_computation.8 | async-start | bytes 8388608
  99.4 14.3 %slice-start.1 = ((s8[8388608]{0:T(1024)(128)(4,1)}), s8[4194304]{0:T(1024)(128)(4,1)S(1)}, s32[]{:S(2)}) async-start(s8[8388608]{0:T(1024)(128)(4,1)} %bitcast.113), calls=%async_computation.9 | async-start | bytes 8388608
  128.0 18.9 %slice-start.2 = ((s8[8388608]{0:T(1024)(128)(4,1)}), s8[4194304]{0:T(1024)(128)(4,1)S(1)}, s32[]{:S(2)}) async-start(s8[8388608]{0:T(1024)(128)(4,1)} %bitcast.115), calls=%async_computation.10 | async-start | bytes 8388608
  132.8 14.1 %slice-start.3 = ((s8[8388608]{0:T(1024)(128)(4,1)}), s8[4194304]{0:T(1024)(128)(4,1)S(1)}, s32[]{:S(2)}) async-start(s8[8388608]{0:T(1024)(128)(4,1)} %bitcast.115), calls=%async_computation.11 | async-start | bytes 8388608
  161.2 19.3 %slice-start.4 = ((s8[8388608]{0:T(1024)(128)(4,1)}), s8[4194304]{0:T(1024)(128)(4,1)S(1)}, s32[]{:S(2)}) async-start(s8[8388608]{0:T(1024)(128)(4,1)} %bitcast.117), calls=%async_computation.12 | async-start | bytes 8388608
  166.0 14.5 %slice-start.5 = ((s8[8388608]{0:T(1024)(128)(4,1)}), s8[4194304]{0:T(1024)(128)(4,1)S(1)}, s32[]{:S(2)}) async-start(s8[8388608]{0:T(1024)(128)(4,1)} %bitcast.117), calls=%async_computation.13 | async-start | bytes 8388608
  194.8 18.9 %slice-start.6 = ((s8[8388608]{0:T(1024)(128)(4,1)}), s8[4194304]{0:T(1024)(128)(4,1)S(1)}, s32[]{:S(2)}) async-start(s8[8388608]{0:T(1024)(128)(4,1)} %bitcast.119), calls=%async_computation.14 | async-start | bytes 8388608
  199.6 14.1 %slice-start.7 = ((s8[8388608]{0:T(1024)(128)(4,1)}), s8[4194304]{0:T(1024)(128)(4,1)S(1)}, s32[]{:S(2)}) async-start(s8[8388608]{0:T(1024)(128)(4,1)} %bitcast.119), calls=%async_computation.15 | async-start | bytes 8388608
  228.0 19.0 %slice-start.8 = ((s8[8388608]{0:T(1024)(128)(4,1)}), s8[4194304]{0:T(1024)(128)(4,1)S(1)}, s32[]{:S(2)}) async-start(s8[8388608]{0:T(1024)(128)(4,1)} %bitcast.121), calls=%async_computation.16 | async-start | bytes 8388608
  232.7 14.3 %slice-start.9 = ((s8[8388608]{0:T(1024)(128)(4,1)}), s8[4194304]{0:T(1024)(128)(4,1)S(1)}, s32[]{:S(2)}) async-start(s8[8388608]{0:T(1024)(128)(4,1)} %bitcast.121), calls=%async_computation.17 | async-start | bytes 8388608
  261.3 18.9 %slice-start.10 = ((s8[8388608]{0:T(1024)(128)(4,1)}), s8[4194304]{0:T(1024)(128)(4,1)S(1)}, s32[]{:S(2)}) async-start(s8[8388608]{0:T(1024)(128)(4,1)} %bitcast.123), calls=%async_computation.18 | async-start | bytes 8388608
  266.1 14.1 %slice-start.11 = ((s8[8388608]{0:T(1024)(128)(4,1)}), s8[4194304]{0:T(1024)(128)(4,1)S(1)}, s32[]{:S(2)}) async-start(s8[8388608]{0:T(1024)(128)(4,1)} %bitcast.123), calls=%async_computation.19 | async-start | bytes 8388608
  283.9 17.3 %copy-start.3 = (f32[40,1024]{1,0:T(8,128)S(1)}, f32[40,1024]{1,0:T(8,128)}, u32[]{:S(2)}) copy-start(f32[40,1024]{1,0:T(8,128)} %param.25) | copy-start | bytes 491524
  299.3 1.9 copy-start.2
  302.8 61.3 %reduce-scatter.7.cloned.1.call-start = ((), (), s32[]{:S(2)}) async-start(), calls=%async_computation.5 | async-start | bytes 409600 | tf_op jit(solution)/shard_map/reduce_scatter | solution.py:117
  325.2 118.3 %copy-start.4 = (f32[40,512]{1,0:T(8,128)S(1)}, f32[40,512]{1,0:T(8,128)}, u32[]{:S(2)}) copy-start(f32[40,512]{1,0:T(8,128)} %reduce-scatter.5.cloned.1.call-done) | copy-start | bytes 245764
  325.2 6.0 %collective-permute-start.1 = (bf16[40,512]{1,0:T(8,128)(2,1)S(1)}, bf16[40,512]{1,0:T(8,128)(2,1)S(1)}, u32[]{:S(2)}, u32[]{:S(2)}) collective-permute-start(bf16[40,512]{1,0:T(8,128)(2,1)S(1)} %select_convert_fusion.2), channel_id=1, source_target_pairs={{8,0},{16,8},{24,16},{9,1},{17,9},{25,17},{10,2},{18,10},{26,18},{... | collective-permute-start | bytes 122888 | tf_op jit(solution)/shard_map/ppermute | solution.py:26
  344.4 59.5 %reduce-scatter.9.cloned.1.call-start = ((), (), s32[]{:S(2)}) async-start(), calls=%async_computation.6 | async-start | bytes 409600 | tf_op jit(solution)/shard_map/reduce_scatter | solution.py:117
  364.1 79.4 %copy-start.5 = (f32[40,512]{1,0:T(8,128)S(1)}, f32[40,512]{1,0:T(8,128)}, u32[]{:S(2)}) copy-start(f32[40,512]{1,0:T(8,128)} %reduce-scatter.7.cloned.1.call-done) | copy-start | bytes 245764
  365.0 5.9 %collective-permute-start.2 = (bf16[40,512]{1,0:T(8,128)(2,1)S(1)}, bf16[40,512]{1,0:T(8,128)(2,1)S(1)}, u32[]{:S(2)}, u32[]{:S(2)}) collective-permute-start(bf16[40,512]{1,0:T(8,128)(2,1)S(1)} %select_convert_fusion.1), channel_id=1, source_target_pairs={{8,0},{16,8},{24,16},{9,1},{17,9},{25,17},{10,2},{18,10},{26,18},{... | collective-permute-start | bytes 122888 | tf_op jit(solution)/shard_map/ppermute | solution.py:26
  384.3 59.2 %reduce-scatter.11.cloned.1.call-start = ((), (), s32[]{:S(2)}) async-start(), calls=%async_computation.7 | async-start | bytes 409600 | tf_op jit(solution)/shard_map/reduce_scatter | solution.py:117
  404.8 5.9 %collective-permute-start.3 = (bf16[40,512]{1,0:T(8,128)(2,1)S(1)}, bf16[40,512]{1,0:T(8,128)(2,1)S(1)}, u32[]{:S(2)}, u32[]{:S(2)}) collective-permute-start(bf16[40,512]{1,0:T(8,128)(2,1)S(1)} %select_convert_fusion), channel_id=1, source_target_pairs={{8,0},{16,8},{24,16},{9,1},{17,9},{25,17},{10,2},{18,10},{26,18},{... | collective-permute-start | bytes 122888 | tf_op jit(solution)/shard_map/ppermute | solution.py:26
Sparse Core Ops, SparseCore 0:
  302.9 21.3 reduce-scatter.4
  344.6 19.4 reduce-scatter.6
  384.4 19.4 reduce-scatter.8
  424.0 19.4 reduce-scatter.10
